TPU v7x, 512 devices: a whole 4x4x16 slice. The times are simulated.
512 devices in a mesh: adapter: 64 (over y, z), mp: 8 (over x, core).
Axes of the slice: x: 4, y: 4, z: 16, core: 2. Of those that a mesh axis runs over, the one named last changes fastest.
Arguments:
- tokens: bfloat16 [24576, 8192], P('adapter', 'mp'), may hold values from -6 to 6
- cotangent: bfloat16 [24576, 1024], P('adapter', 'mp'), may hold values from -6 to 6
- value_weight: bfloat16 [8192, 1024], P('mp', 'adapter'), may hold values from -0.0625 to 0.0625
- down_store: bfloat16 [128, 8, 1024, 64], P(None, 'mp', 'adapter'), may hold values from -0.0625 to 0.0625
- down_first: float32 [128, 8, 1024, 64], P(None, 'mp', 'adapter'), may hold values from -4 to 4
- down_second: float32 [128, 8, 1024, 64], P(None, 'mp', 'adapter'), may hold values from 0.01 to 1
- up_store: bfloat16 [128, 64, 1024], P(None, 'adapter', 'mp'), may hold values from -0.75 to 0.75
- up_first: float32 [128, 64, 1024], P(None, 'adapter', 'mp'), may hold values from -4 to 4
- up_second: float32 [128, 64, 1024], P(None, 'adapter', 'mp'), may hold values from 0.01 to 1
- tile_adapter: int32 [192], replicated, may hold values from 0 to 127
- tile_length: int32 [192], replicated, may hold values from 1 to 128, as said below
- adapter_slot: int32 [128], replicated, may hold values from 0 to 127, each once
Outputs:
- projected: bfloat16 [24576, 1024], P('adapter', 'mp')
- token_gradient: bfloat16 [24576, 8192], P('adapter', 'mp')
- new_down: float32 [128, 8, 1024, 64], P(None, 'mp', 'adapter')
- new_down_first: float32 [128, 8, 1024, 64], P(None, 'mp', 'adapter')
- new_down_second: float32 [128, 8, 1024, 64], P(None, 'mp', 'adapter')
- new_up: float32 [128, 64, 1024], P(None, 'adapter', 'mp')
- new_up_first: float32 [128, 64, 1024], P(None, 'adapter', 'mp')
- new_up_second: float32 [128, 64, 1024], P(None, 'adapter', 'mp')
Inputs may be any that keep to these rules, and one draw needn't show every extreme that they name: `tile_length`: some tile is full in every draw. `adapter_slot`: each slot holds exactly one adapter.
All inputs are finite; a program needn't handle non-finite values.
Results may differ from a plain program's by a relative error of at most 0.0046.
Values may be sent and summed in bfloat16 or wider, within the bound.
No kernel may reach another device: no remote copies, remote signals or barrier semaphores. Data moves between devices by JAX's collectives and lax.ppermute only.
A program may use at most 64 MiB of HBM per device.

v0:
```python
import jax
import jax.numpy as jnp
from jax import lax
from jax.sharding import Mesh, PartitionSpec as P

TILE = 128
STEP = 100
adapter_scale = 2.0
learn_rate = 0.001
beta_one = 0.9
beta_two = 0.999
adam_eps = 1e-08


def adam_step(store, first, second, gradient):
    new_first = beta_one * first + (1.0 - beta_one) * gradient
    new_second = beta_two * second + (1.0 - beta_two) * gradient * gradient
    corr_one = 1.0 - beta_one**STEP
    corr_two = 1.0 - beta_two**STEP
    moved = store.astype(jnp.float32) - learn_rate * (new_first / corr_one) / (
        jnp.sqrt(new_second / corr_two) + adam_eps
    )
    return (moved, new_first, new_second)


ADAPTER = ("ay", "az")


def gather_along(piece, axis):
    count = lax.axis_size(axis)
    got = [piece]
    for shift in range(1, count):
        pairs = [(j, (j - shift) % count) for j in range(count)]
        got.append(lax.ppermute(piece, axis, pairs))
    ordered = jnp.roll(jnp.stack(got), lax.axis_index(axis), axis=0)
    return jnp.moveaxis(ordered, 0, 1).reshape(piece.shape[0], count * piece.shape[1])


def gather_weight(value_weight):
    return gather_along(gather_along(value_weight, "az"), "ay")


def split_adapter(mesh):
    devices = mesh.devices
    n_adapter = devices.shape[0]
    try:
        n_y = len({d.coords[1] for d in devices[:, 0]})
    except (AttributeError, IndexError, TypeError):
        n_y = 1
    if n_y < 1 or n_adapter % n_y:
        n_y = 1
    return Mesh(devices.reshape(n_y, n_adapter // n_y, devices.shape[1]), ("ay", "az", "mp"))


def shards(
    tokens,
    cotangent,
    value_weight,
    down_store,
    down_first,
    down_second,
    up_store,
    up_first,
    up_second,
    tile_adapter,
    tile_length,
    adapter_slot,
):
    tile_total = tile_adapter.shape[0]
    tok_count, feat_part = tokens.shape
    head_cols = cotangent.shape[1]
    tiles_here = tok_count // TILE
    adapter_count = adapter_slot.shape[0]
    my_index = lax.axis_index(ADAPTER)
    adapter_ids = jnp.arange(adapter_count, dtype=jnp.int32)
    tile_adapter_slot = jnp.sum(
        jnp.where(tile_adapter[:, None] == adapter_ids[None, :], adapter_slot[None, :], 0), axis=1
    )
    my_lengths = lax.dynamic_slice_in_dim(tile_length, my_index * tiles_here, tiles_here)
    active_rows = (jnp.arange(TILE)[None, :] < my_lengths[:, None]).reshape(tok_count, 1)
    masked_own = cotangent * active_rows.astype(jnp.bfloat16)
    masked_full = lax.all_gather(masked_own, "mp", axis=1, tiled=True)
    n_adapter = tile_total // tiles_here
    row_part = down_store.shape[2]
    rank = down_store.shape[3]
    sent_down = down_store[:, 0][tile_adapter_slot].reshape(tile_total, row_part * rank)
    sent_up = up_store[tile_adapter_slot].reshape(tile_total, head_cols)
    sent = jnp.concatenate([sent_down, sent_up], axis=1)
    arrived = lax.all_to_all(sent, ADAPTER, split_axis=0, concat_axis=0, tiled=True)
    arrived = arrived.reshape(n_adapter, tiles_here, row_part * rank + head_cols)
    down_panel = (
        arrived[:, :, : row_part * rank]
        .reshape(n_adapter, tiles_here, row_part, rank)
        .transpose(1, 0, 2, 3)
        .reshape(tiles_here, n_adapter * row_part, rank)
    )
    up_panel = arrived[:, :, row_part * rank :].transpose(1, 0, 2)
    w_full = gather_weight(value_weight)
    token_tiles = tokens.reshape(tiles_here, TILE, feat_part)
    frozen_part = jnp.dot(tokens, w_full, preferred_element_type=jnp.float32)
    frozen_local = lax.psum_scatter(frozen_part, "mp", scatter_dimension=1, tiled=True)
    down_part = jnp.einsum(
        "ntd,ndr->ntr", token_tiles, down_panel, preferred_element_type=jnp.float32
    )
    down_sum = lax.psum(down_part, "mp")
    down_portion = down_sum.astype(jnp.bfloat16)
    adapter_term = jnp.einsum(
        "ntr,nrv->ntv", down_portion, up_panel, preferred_element_type=jnp.float32
    ).reshape(tok_count, head_cols)
    projected = (
        (frozen_local + adapter_scale * adapter_term) * active_rows.astype(jnp.float32)
    ).astype(jnp.bfloat16)
    tile_mask = masked_own.reshape(tiles_here, TILE, head_cols)
    backward_piece = adapter_scale * jnp.einsum(
        "ntv,nrv->ntr", tile_mask, up_panel, preferred_element_type=jnp.float32
    )
    backward_portion = lax.psum(backward_piece, "mp").astype(jnp.bfloat16)
    frozen_backward = lax.dot_general(
        masked_full, w_full, (((1,), (1,)), ((), ())), preferred_element_type=jnp.float32
    )
    adapter_backward = jnp.einsum(
        "ntr,ndr->ntd", backward_portion, down_panel, preferred_element_type=jnp.float32
    ).reshape(tok_count, feat_part)
    token_gradient = (frozen_backward + adapter_backward).astype(jnp.bfloat16)
    home_down = jnp.einsum(
        "ntd,ntr->ndr", token_tiles, backward_portion, preferred_element_type=jnp.float32
    )
    local_up_weight = adapter_scale * jnp.einsum(
        "ntr,ntv->nrv", down_portion, tile_mask, preferred_element_type=jnp.float32
    )
    grads = jnp.concatenate(
        [home_down.reshape(tiles_here, n_adapter, row_part * rank), local_up_weight], axis=2
    )
    grads = lax.all_to_all(grads, ADAPTER, split_axis=1, concat_axis=0, tiled=True)
    arrived_down = grads[:, 0, : row_part * rank]
    arrived_up = grads[:, 0, row_part * rank :]
    selector = (adapter_ids[:, None] == tile_adapter_slot[None, :]).astype(jnp.float32)
    down_gradient = jnp.dot(
        selector, arrived_down.reshape(tile_total, -1), precision=lax.Precision.HIGHEST
    ).reshape(down_store.shape)
    up_gradient = jnp.dot(
        selector, arrived_up.reshape(tile_total, -1), precision=lax.Precision.HIGHEST
    ).reshape(up_store.shape)
    new_down, new_down_first, new_down_second = adam_step(
        down_store, down_first, down_second, down_gradient
    )
    new_up, new_up_first, new_up_second = adam_step(up_store, up_first, up_second, up_gradient)
    return (
        projected,
        token_gradient,
        new_down,
        new_down_first,
        new_down_second,
        new_up,
        new_up_first,
        new_up_second,
    )


def solution(mesh):
    mesh = split_adapter(mesh)
    placed = (
        P(ADAPTER, "mp"),
        P(ADAPTER, "mp"),
        P("mp", ADAPTER),
        P(None, "mp", ADAPTER, None),
        P(None, "mp", ADAPTER, None),
        P(None, "mp", ADAPTER, None),
        P(None, ADAPTER, "mp"),
        P(None, ADAPTER, "mp"),
        P(None, ADAPTER, "mp"),
        P(),
        P(),
        P(),
    )
    return jax.shard_map(
        shards,
        mesh=mesh,
        in_specs=placed,
        out_specs=(
            P(ADAPTER, "mp"),
            P(ADAPTER, "mp"),
            P(None, "mp", ADAPTER, None),
            P(None, "mp", ADAPTER, None),
            P(None, "mp", ADAPTER, None),
            P(None, ADAPTER, "mp"),
            P(None, ADAPTER, "mp"),
            P(None, ADAPTER, "mp"),
        ),
        check_vma=False,
    )
```

profile of v0, /device:TPU:6, one launch (start us, length us, event | category | flops | bytes accessed | tf_op | source)
XLA Modules:
  0.0 261.7 jit_solution(3475305058610863027)
XLA Ops:
  7.2 11.5 %collective-permute-start = (bf16[1024,16]{0,1:T(8,128)(2,1)}, bf16[1024,16]{0,1:T(8,128)(2,1)S(1)}, u32[]{:S(2)}, u32[]{:S(2)}) collective-permute-start(bf16[1024,16]{0,1:T(8,128)(2,1)} %param.14), channel_id=1, source_target_pairs={{0,120},{8,0},{16,8},{24,16},{32,24},{40,32},{48,40},{56,48},{64,5... | collective-permute-start | bytes 98312 | tf_op jit(solution)/shard_map/ppermute | solution.py:34
  18.7 3.4 %collective-permute-start.1 = (bf16[1024,16]{0,1:T(8,128)(2,1)}, bf16[1024,16]{0,1:T(8,128)(2,1)S(1)}, u32[]{:S(2)}, u32[]{:S(2)}) collective-permute-start(bf16[1024,16]{0,1:T(8,128)(2,1)} %param.14), channel_id=1, source_target_pairs={{0,112},{8,120},{16,0},{24,8},{32,16},{40,24},{48,32},{56,40},{64,... | collective-permute-start | bytes 98312 | tf_op jit(solution)/shard_map/ppermute | solution.py:34
  22.1 5.0 %collective-permute-start.2 = (bf16[1024,16]{0,1:T(8,128)(2,1)}, bf16[1024,16]{0,1:T(8,128)(2,1)S(1)}, u32[]{:S(2)}, u32[]{:S(2)}) collective-permute-start(bf16[1024,16]{0,1:T(8,128)(2,1)} %param.14), channel_id=1, source_target_pairs={{0,104},{8,112},{16,120},{24,0},{32,8},{40,16},{48,24},{56,32},{64... | collective-permute-start | bytes 98312 | tf_op jit(solution)/shard_map/ppermute | solution.py:34
  27.1 2.8 %collective-permute-start.3 = (bf16[1024,16]{0,1:T(8,128)(2,1)}, bf16[1024,16]{0,1:T(8,128)(2,1)S(1)}, u32[]{:S(2)}, u32[]{:S(2)}) collective-permute-start(bf16[1024,16]{0,1:T(8,128)(2,1)} %param.14), channel_id=1, source_target_pairs={{0,96},{8,104},{16,112},{24,120},{32,0},{40,8},{48,16},{56,24},{64... | collective-permute-start | bytes 98312 | tf_op jit(solution)/shard_map/ppermute | solution.py:34
  30.0 1.9 collective-permute-start.4
  38.1 15.8 %all-to-all-start = ((bf16[64,3,1152]{2,1,0:T(4,128)(2,1)}), bf16[64,3,1152]{2,1,0:T(4,128)(2,1)S(1)}, u32[]{:S(2)}, u32[]{:S(2)}) async-start(bf16[64,3,1152]{2,1,0:T(4,128)(2,1)} %pad_maximum_fusion.1), calls=%async_computation.1 | async-start | bytes 1179648 | tf_op jit(solution)/shard_map/all_to_all | solution.py:89
  54.0 10.4 %collective-permute-start.5 = (bf16[1024,16]{0,1:T(8,128)(2,1)S(1)}, bf16[1024,16]{0,1:T(8,128)(2,1)S(1)}, u32[]{:S(2)}, u32[]{:S(2)}) collective-permute-start(bf16[1024,16]{0,1:T(8,128)(2,1)S(1)} %copy-done.3), channel_id=1, source_target_pairs={{0,80},{8,88},{16,96},{24,104},{32,112},{40,120},{48,0},{56,8},{64... | collective-permute-start | bytes 98312 | tf_op jit(solution)/shard_map/ppermute | solution.py:34
  64.4 4.3 %collective-permute-start.6 = (bf16[1024,16]{0,1:T(8,128)(2,1)S(1)}, bf16[1024,16]{0,1:T(8,128)(2,1)S(1)}, u32[]{:S(2)}, u32[]{:S(2)}) collective-permute-start(bf16[1024,16]{0,1:T(8,128)(2,1)S(1)} %copy-done.3), channel_id=1, source_target_pairs={{0,72},{8,80},{16,88},{24,96},{32,104},{40,112},{48,120},{56,0},{6... | collective-permute-start | bytes 98312 | tf_op jit(solution)/shard_map/ppermute | solution.py:34
  68.7 9.4 %collective-permute-start.7 = (bf16[1024,16]{0,1:T(8,128)(2,1)S(1)}, bf16[1024,16]{0,1:T(8,128)(2,1)S(1)}, u32[]{:S(2)}, u32[]{:S(2)}) collective-permute-start(bf16[1024,16]{0,1:T(8,128)(2,1)S(1)} %copy-done.3), channel_id=1, source_target_pairs={{0,64},{8,72},{16,80},{24,88},{32,96},{40,104},{48,112},{56,120},{... | collective-permute-start | bytes 98312 | tf_op jit(solution)/shard_map/ppermute | solution.py:34
  78.1 3.1 %collective-permute-start.8 = (bf16[1024,16]{0,1:T(8,128)(2,1)S(1)}, bf16[1024,16]{0,1:T(8,128)(2,1)S(1)}, u32[]{:S(2)}, u32[]{:S(2)}) collective-permute-start(bf16[1024,16]{0,1:T(8,128)(2,1)S(1)} %copy-done.3), channel_id=1, source_target_pairs={{0,56},{8,64},{16,72},{24,80},{32,88},{40,96},{48,104},{56,112},{6... | collective-permute-start | bytes 98312 | tf_op jit(solution)/shard_map/ppermute | solution.py:34
  81.2 10.3 %collective-permute-start.9 = (bf16[1024,16]{0,1:T(8,128)(2,1)S(1)}, bf16[1024,16]{0,1:T(8,128)(2,1)S(1)}, u32[]{:S(2)}, u32[]{:S(2)}) collective-permute-start(bf16[1024,16]{0,1:T(8,128)(2,1)S(1)} %copy-done.3), channel_id=1, source_target_pairs={{0,48},{8,56},{16,64},{24,72},{32,80},{40,88},{48,96},{56,104},{64... | collective-permute-start | bytes 98312 | tf_op jit(solution)/shard_map/ppermute | solution.py:34
  91.5 6.7 %collective-permute-start.10 = (bf16[1024,16]{0,1:T(8,128)(2,1)S(1)}, bf16[1024,16]{0,1:T(8,128)(2,1)S(1)}, u32[]{:S(2)}, u32[]{:S(2)}) collective-permute-start(bf16[1024,16]{0,1:T(8,128)(2,1)S(1)} %copy-done.3), channel_id=1, source_target_pairs={{0,40},{8,48},{16,56},{24,64},{32,72},{40,80},{48,88},{56,96},{64,... | collective-permute-start | bytes 98312 | tf_op jit(solution)/shard_map/ppermute | solution.py:34
  98.2 1.9 collective-permute-start.11
  100.2 5.2 %collective-permute-start.12 = (bf16[1024,16]{0,1:T(8,128)(2,1)S(1)}, bf16[1024,16]{0,1:T(8,128)(2,1)S(1)}, u32[]{:S(2)}, u32[]{:S(2)}) collective-permute-start(bf16[1024,16]{0,1:T(8,128)(2,1)S(1)} %copy-done.3), channel_id=1, source_target_pairs={{0,24},{8,32},{16,40},{24,48},{32,56},{40,64},{48,72},{56,80},{64,... | collective-permute-start | bytes 98312 | tf_op jit(solution)/shard_map/ppermute | solution.py:34
  105.5 2.7 %collective-permute-start.13 = (bf16[1024,16]{0,1:T(8,128)(2,1)S(1)}, bf16[1024,16]{0,1:T(8,128)(2,1)S(1)}, u32[]{:S(2)}, u32[]{:S(2)}) collective-permute-start(bf16[1024,16]{0,1:T(8,128)(2,1)S(1)} %copy-done.3), channel_id=1, source_target_pairs={{0,16},{8,24},{16,32},{24,40},{32,48},{40,56},{48,64},{56,72},{64,... | collective-permute-start | bytes 98312 | tf_op jit(solution)/shard_map/ppermute | solution.py:34
  108.1 4.8 %collective-permute-start.14 = (bf16[1024,16]{0,1:T(8,128)(2,1)S(1)}, bf16[1024,16]{0,1:T(8,128)(2,1)S(1)}, u32[]{:S(2)}, u32[]{:S(2)}) collective-permute-start(bf16[1024,16]{0,1:T(8,128)(2,1)S(1)} %copy-done.3), channel_id=1, source_target_pairs={{0,8},{8,16},{16,24},{24,32},{32,40},{40,48},{48,56},{56,64},{64,7... | collective-permute-start | bytes 98312 | tf_op jit(solution)/shard_map/ppermute | solution.py:34
  113.4 1.8 collective-permute-done.14
  115.4 4.8 %collective-permute-start.15 = (bf16[1024,256]{0,1:T(8,128)(2,1)S(1)}, bf16[1024,256]{0,1:T(8,128)(2,1)S(1)}, u32[]{:S(2)}, u32[]{:S(2)}) collective-permute-start(bf16[1024,256]{0,1:T(8,128)(2,1)S(1)} %bitcast.143), channel_id=1, source_target_pairs={{0,384},{128,0},{256,128},{384,256},{1,385},{129,1},{257,129},{385... | collective-permute-start | bytes 1572872 | tf_op jit(solution)/shard_map/ppermute | solution.py:34
  120.3 2.5 collective-permute-start.16
  123.0 2.9 %collective-permute-start.17 = (bf16[1024,256]{0,1:T(8,128)(2,1)S(1)}, bf16[1024,256]{0,1:T(8,128)(2,1)S(1)}, u32[]{:S(2)}, u32[]{:S(2)}) collective-permute-start(bf16[1024,256]{0,1:T(8,128)(2,1)S(1)} %bitcast.145), channel_id=1, source_target_pairs={{0,128},{128,256},{256,384},{384,0},{1,129},{129,257},{257,385},{3... | collective-permute-start | bytes 1572872 | tf_op jit(solution)/shard_map/ppermute | solution.py:34
  125.9 11.5 %collective-permute-done.15 = bf16[1024,256]{0,1:T(8,128)(2,1)S(1)} collective-permute-done((bf16[1024,256]{0,1:T(8,128)(2,1)S(1)}, bf16[1024,256]{0,1:T(8,128)(2,1)S(1)}, u32[]{:S(2)}, u32[]{:S(2)}) %collective-permute-start.15) | collective-permute-done | bytes 524320 | tf_op jit(solution)/shard_map/ppermute | solution.py:34
  137.6 5.5 %collective-permute-done.17 = bf16[1024,256]{0,1:T(8,128)(2,1)S(1)} collective-permute-done((bf16[1024,256]{0,1:T(8,128)(2,1)S(1)}, bf16[1024,256]{0,1:T(8,128)(2,1)S(1)}, u32[]{:S(2)}, u32[]{:S(2)}) %collective-permute-start.17) | collective-permute-done | bytes 524320 | tf_op jit(solution)/shard_map/ppermute | solution.py:34
  146.4 22.7 %all-reduce.2 = (bf16[3,128,64]{1,2,0:T(8,128)(2,1)S(1)}, bf16[3,128,64]{1,2,0:T(8,128)(2,1)S(1)}) all-reduce(f32[3,128,64]{1,2,0:T(8,128)S(1)} %convolution_bitcast_fusion.2, f32[3,128,64]{1,2,0:T(8,128)S(1)} %convolution_multiply_fusion.2), channel_id=1, replica_groups=mesh['ay'=4,'az'=16,'mp'=8] {'mp'}, use_global_device_ids=true, to_apply=%region_2.3 | all-reduce | flops 49152 | bytes 294912 | tf_op jit(solution)/shard_map/psum | solution.py:105
  176.1 10.2 %all-to-all-start.1 = ((f32[3,64,1152]{2,0,1:T(4,128)}), f32[3,64,1152]{2,0,1:T(4,128)S(1)}, u32[]{:S(2)}, u32[]{:S(2)}) async-start(f32[3,64,1152]{2,0,1:T(4,128)} %copy.83), calls=%async_computation.2 | async-start | bytes 2359296 | tf_op jit(solution)/shard_map/all_to_all | solution.py:134
  186.4 4.0 %convolution_bitcast_fusion = f32[384,1024]{0,1:T(8,128)} fusion(bf16[1024,1024]{0,1:T(8,128)(2,1)} %bitcast.150, bf16[384,1024]{1,0:T(8,128)(2,1)S(1)} %copy-done), kind=kOutput, calls=%fused_computation.4 | convolution fusion | flops 805306368 | bytes 4456448 | tf_op jit(solution)/shard_map/dot_general | solution.py:100
  190.4 15.3 %all_gather.3 = bf16[384,1024]{1,0:T(8,128)(2,1)} all-gather(bf16[384,128]{1,0:T(8,128)(2,1)S(1)} %broadcast_multiply_fusion), channel_id=1, replica_groups=mesh['ay'=4,'az'=16,'mp'=8] {'mp'}, dimensions={1}, use_global_device_ids=true | all-gather | bytes 884736 | tf_op jit(solution)/shard_map/all_gather | solution.py:82
  206.5 3.7 %fusion = bf16[384,1024]{1,0:T(8,128)(2,1)} fusion(f32[3,128,1024]{2,1,0:T(8,128)S(1)} %fusion.19, bf16[384,1024]{1,0:T(8,128)(2,1)} %all_gather.3, bf16[1024,1024]{0,1:T(8,128)(2,1)} %bitcast.151), kind=kOutput, calls=%fused_computation.3 | convolution fusion | flops 806092800 | bytes 5242880 | tf_op jit(solution)/shard_map/dot_general | solution.py:118
  210.2 19.9 %reduce-scatter.2.cloned.1.call-done = f32[384,128]{0,1:T(8,128)} async-done(((f32[384,1024]{0,1:T(8,128)}), f32[384,128]{0,1:T(8,128)}) %reduce-scatter.2.cloned.1.call-update) | async-done | bytes 196624 | tf_op jit(solution)/shard_map/reduce_scatter | solution.py:101
  231.8 14.7 %all-to-all-done.1 = f32[3,64,1152]{2,0,1:T(4,128)S(1)} async-done(((f32[3,64,1152]{2,0,1:T(4,128)}), f32[3,64,1152]{2,0,1:T(4,128)S(1)}, u32[]{:S(2)}, u32[]{:S(2)}) %all-to-all-start.1) | async-done | bytes 884768 | tf_op jit(solution)/shard_map/all_to_all | solution.py:134
  246.5 2.1 all_to_all.21
  248.6 1.7 slice.22
  251.3 2.6 divide_subtract_fusion
  (109 shorter events, 21.9 us)
Async XLA Ops:
  7.2 138.8 %copy-start = (bf16[384,1024]{1,0:T(8,128)(2,1)S(1)}, bf16[384,1024]{1,0:T(8,128)(2,1)}, u32[]{:S(2)}) copy-start(bf16[384,1024]{1,0:T(8,128)(2,1)} %param.12) | copy-start | bytes 2359300
  7.2 46.7 %copy-start.3 = (bf16[1024,16]{0,1:T(8,128)(2,1)S(1)}, bf16[1024,16]{0,1:T(8,128)(2,1)}, u32[]{:S(2)}) copy-start(bf16[1024,16]{0,1:T(8,128)(2,1)} %param.14) | copy-start | bytes 98308
  7.2 46.7 %copy-start.7 = (s32[192]{0:T(256)S(1)}, s32[192]{0:T(256)}, u32[]{:S(2)}) copy-start(s32[192]{0:T(256)} %param.22) | copy-start | bytes 2308
  7.2 46.8 %collective-permute-start = (bf16[1024,16]{0,1:T(8,128)(2,1)}, bf16[1024,16]{0,1:T(8,128)(2,1)S(1)}, u32[]{:S(2)}, u32[]{:S(2)}) collective-permute-start(bf16[1024,16]{0,1:T(8,128)(2,1)} %param.14), channel_id=1, source_target_pairs={{0,120},{8,0},{16,8},{24,16},{32,24},{40,32},{48,40},{56,48},{64,5... | collective-permute-start | bytes 98312 | tf_op jit(solution)/shard_map/ppermute | solution.py:34
  18.7 45.6 %collective-permute-start.1 = (bf16[1024,16]{0,1:T(8,128)(2,1)}, bf16[1024,16]{0,1:T(8,128)(2,1)S(1)}, u32[]{:S(2)}, u32[]{:S(2)}) collective-permute-start(bf16[1024,16]{0,1:T(8,128)(2,1)} %param.14), channel_id=1, source_target_pairs={{0,112},{8,120},{16,0},{24,8},{32,16},{40,24},{48,32},{56,40},{64,... | collective-permute-start | bytes 98312 | tf_op jit(solution)/shard_map/ppermute | solution.py:34
  22.1 46.6 %collective-permute-start.2 = (bf16[1024,16]{0,1:T(8,128)(2,1)}, bf16[1024,16]{0,1:T(8,128)(2,1)S(1)}, u32[]{:S(2)}, u32[]{:S(2)}) collective-permute-start(bf16[1024,16]{0,1:T(8,128)(2,1)} %param.14), channel_id=1, source_target_pairs={{0,104},{8,112},{16,120},{24,0},{32,8},{40,16},{48,24},{56,32},{64... | collective-permute-start | bytes 98312 | tf_op jit(solution)/shard_map/ppermute | solution.py:34
  27.1 51.0 %collective-permute-start.3 = (bf16[1024,16]{0,1:T(8,128)(2,1)}, bf16[1024,16]{0,1:T(8,128)(2,1)S(1)}, u32[]{:S(2)}, u32[]{:S(2)}) collective-permute-start(bf16[1024,16]{0,1:T(8,128)(2,1)} %param.14), channel_id=1, source_target_pairs={{0,96},{8,104},{16,112},{24,120},{32,0},{40,8},{48,16},{56,24},{64... | collective-permute-start | bytes 98312 | tf_op jit(solution)/shard_map/ppermute | solution.py:34
  30.0 51.2 %collective-permute-start.4 = (bf16[1024,16]{0,1:T(8,128)(2,1)}, bf16[1024,16]{0,1:T(8,128)(2,1)S(1)}, u32[]{:S(2)}, u32[]{:S(2)}) collective-permute-start(bf16[1024,16]{0,1:T(8,128)(2,1)} %param.14), channel_id=1, source_target_pairs={{0,88},{8,96},{16,104},{24,112},{32,120},{40,0},{48,8},{56,16},{64... | collective-permute-start | bytes 98312 | tf_op jit(solution)/shard_map/ppermute | solution.py:34
  34.2 88.7 %copy-start.4 = (bf16[384,128]{1,0:T(8,128)(2,1)S(1)}, bf16[384,128]{1,0:T(8,128)(2,1)}, u32[]{:S(2)}) copy-start(bf16[384,128]{1,0:T(8,128)(2,1)} %param.13) | copy-start | bytes 294916
  38.1 106.8 %all-to-all-start = ((bf16[64,3,1152]{2,1,0:T(4,128)(2,1)}), bf16[64,3,1152]{2,1,0:T(4,128)(2,1)S(1)}, u32[]{:S(2)}, u32[]{:S(2)}) async-start(bf16[64,3,1152]{2,1,0:T(4,128)(2,1)} %pad_maximum_fusion.1), calls=%async_computation.1 | async-start | bytes 1179648 | tf_op jit(solution)/shard_map/all_to_all | solution.py:89
  54.0 37.5 %collective-permute-start.5 = (bf16[1024,16]{0,1:T(8,128)(2,1)S(1)}, bf16[1024,16]{0,1:T(8,128)(2,1)S(1)}, u32[]{:S(2)}, u32[]{:S(2)}) collective-permute-start(bf16[1024,16]{0,1:T(8,128)(2,1)S(1)} %copy-done.3), channel_id=1, source_target_pairs={{0,80},{8,88},{16,96},{24,104},{32,112},{40,120},{48,0},{56,8},{64... | collective-permute-start | bytes 98312 | tf_op jit(solution)/shard_map/ppermute | solution.py:34
  64.4 33.8 %collective-permute-start.6 = (bf16[1024,16]{0,1:T(8,128)(2,1)S(1)}, bf16[1024,16]{0,1:T(8,128)(2,1)S(1)}, u32[]{:S(2)}, u32[]{:S(2)}) collective-permute-start(bf16[1024,16]{0,1:T(8,128)(2,1)S(1)} %copy-done.3), channel_id=1, source_target_pairs={{0,72},{8,80},{16,88},{24,96},{32,104},{40,112},{48,120},{56,0},{6... | collective-permute-start | bytes 98312 | tf_op jit(solution)/shard_map/ppermute | solution.py:34
  68.7 31.5 %collective-permute-start.7 = (bf16[1024,16]{0,1:T(8,128)(2,1)S(1)}, bf16[1024,16]{0,1:T(8,128)(2,1)S(1)}, u32[]{:S(2)}, u32[]{:S(2)}) collective-permute-start(bf16[1024,16]{0,1:T(8,128)(2,1)S(1)} %copy-done.3), channel_id=1, source_target_pairs={{0,64},{8,72},{16,80},{24,88},{32,96},{40,104},{48,112},{56,120},{... | collective-permute-start | bytes 98312 | tf_op jit(solution)/shard_map/ppermute | solution.py:34
  78.1 27.3 %collective-permute-start.8 = (bf16[1024,16]{0,1:T(8,128)(2,1)S(1)}, bf16[1024,16]{0,1:T(8,128)(2,1)S(1)}, u32[]{:S(2)}, u32[]{:S(2)}) collective-permute-start(bf16[1024,16]{0,1:T(8,128)(2,1)S(1)} %copy-done.3), channel_id=1, source_target_pairs={{0,56},{8,64},{16,72},{24,80},{32,88},{40,96},{48,104},{56,112},{6... | collective-permute-start | bytes 98312 | tf_op jit(solution)/shard_map/ppermute | solution.py:34
  81.2 26.9 %collective-permute-start.9 = (bf16[1024,16]{0,1:T(8,128)(2,1)S(1)}, bf16[1024,16]{0,1:T(8,128)(2,1)S(1)}, u32[]{:S(2)}, u32[]{:S(2)}) collective-permute-start(bf16[1024,16]{0,1:T(8,128)(2,1)S(1)} %copy-done.3), channel_id=1, source_target_pairs={{0,48},{8,56},{16,64},{24,72},{32,80},{40,88},{48,96},{56,104},{64... | collective-permute-start | bytes 98312 | tf_op jit(solution)/shard_map/ppermute | solution.py:34
  91.5 21.4 %collective-permute-start.10 = (bf16[1024,16]{0,1:T(8,128)(2,1)S(1)}, bf16[1024,16]{0,1:T(8,128)(2,1)S(1)}, u32[]{:S(2)}, u32[]{:S(2)}) collective-permute-start(bf16[1024,16]{0,1:T(8,128)(2,1)S(1)} %copy-done.3), channel_id=1, source_target_pairs={{0,40},{8,48},{16,56},{24,64},{32,72},{40,80},{48,88},{56,96},{64,... | collective-permute-start | bytes 98312 | tf_op jit(solution)/shard_map/ppermute | solution.py:34
  98.2 14.7 %collective-permute-start.11 = (bf16[1024,16]{0,1:T(8,128)(2,1)S(1)}, bf16[1024,16]{0,1:T(8,128)(2,1)S(1)}, u32[]{:S(2)}, u32[]{:S(2)}) collective-permute-start(bf16[1024,16]{0,1:T(8,128)(2,1)S(1)} %copy-done.3), channel_id=1, source_target_pairs={{0,32},{8,40},{16,48},{24,56},{32,64},{40,72},{48,80},{56,88},{64,... | collective-permute-start | bytes 98312 | tf_op jit(solution)/shard_map/ppermute | solution.py:34
  100.2 12.8 %collective-permute-start.12 = (bf16[1024,16]{0,1:T(8,128)(2,1)S(1)}, bf16[1024,16]{0,1:T(8,128)(2,1)S(1)}, u32[]{:S(2)}, u32[]{:S(2)}) collective-permute-start(bf16[1024,16]{0,1:T(8,128)(2,1)S(1)} %copy-done.3), channel_id=1, source_target_pairs={{0,24},{8,32},{16,40},{24,48},{32,56},{40,64},{48,72},{56,80},{64,... | collective-permute-start | bytes 98312 | tf_op jit(solution)/shard_map/ppermute | solution.py:34
  105.5 7.9 %collective-permute-start.13 = (bf16[1024,16]{0,1:T(8,128)(2,1)S(1)}, bf16[1024,16]{0,1:T(8,128)(2,1)S(1)}, u32[]{:S(2)}, u32[]{:S(2)}) collective-permute-start(bf16[1024,16]{0,1:T(8,128)(2,1)S(1)} %copy-done.3), channel_id=1, source_target_pairs={{0,16},{8,24},{16,32},{24,40},{32,48},{40,56},{48,64},{56,72},{64,... | collective-permute-start | bytes 98312 | tf_op jit(solution)/shard_map/ppermute | solution.py:34
  108.1 7.0 %collective-permute-start.14 = (bf16[1024,16]{0,1:T(8,128)(2,1)S(1)}, bf16[1024,16]{0,1:T(8,128)(2,1)S(1)}, u32[]{:S(2)}, u32[]{:S(2)}) collective-permute-start(bf16[1024,16]{0,1:T(8,128)(2,1)S(1)} %copy-done.3), channel_id=1, source_target_pairs={{0,8},{8,16},{16,24},{24,32},{32,40},{40,48},{48,56},{56,64},{64,7... | collective-permute-start | bytes 98312 | tf_op jit(solution)/shard_map/ppermute | solution.py:34
  115.4 22.0 %collective-permute-start.15 = (bf16[1024,256]{0,1:T(8,128)(2,1)S(1)}, bf16[1024,256]{0,1:T(8,128)(2,1)S(1)}, u32[]{:S(2)}, u32[]{:S(2)}) collective-permute-start(bf16[1024,256]{0,1:T(8,128)(2,1)S(1)} %bitcast.143), channel_id=1, source_target_pairs={{0,384},{128,0},{256,128},{384,256},{1,385},{129,1},{257,129},{385... | collective-permute-start | bytes 1572872 | tf_op jit(solution)/shard_map/ppermute | solution.py:34
  120.3 17.2 %collective-permute-start.16 = (bf16[1024,256]{0,1:T(8,128)(2,1)S(1)}, bf16[1024,256]{0,1:T(8,128)(2,1)S(1)}, u32[]{:S(2)}, u32[]{:S(2)}) collective-permute-start(bf16[1024,256]{0,1:T(8,128)(2,1)S(1)} %bitcast.144), channel_id=1, source_target_pairs={{0,256},{128,384},{256,0},{384,128},{1,257},{129,385},{257,1},{385... | collective-permute-start | bytes 1572872 | tf_op jit(solution)/shard_map/ppermute | solution.py:34
  123.0 20.1 %collective-permute-start.17 = (bf16[1024,256]{0,1:T(8,128)(2,1)S(1)}, bf16[1024,256]{0,1:T(8,128)(2,1)S(1)}, u32[]{:S(2)}, u32[]{:S(2)}) collective-permute-start(bf16[1024,256]{0,1:T(8,128)(2,1)S(1)} %bitcast.145), channel_id=1, source_target_pairs={{0,128},{128,256},{256,384},{384,0},{1,129},{129,257},{257,385},{3... | collective-permute-start | bytes 1572872 | tf_op jit(solution)/shard_map/ppermute | solution.py:34
  176.1 70.4 %all-to-all-start.1 = ((f32[3,64,1152]{2,0,1:T(4,128)}), f32[3,64,1152]{2,0,1:T(4,128)S(1)}, u32[]{:S(2)}, u32[]{:S(2)}) async-start(f32[3,64,1152]{2,0,1:T(4,128)} %copy.83), calls=%async_computation.2 | async-start | bytes 2359296 | tf_op jit(solution)/shard_map/all_to_all | solution.py:134
  186.3 43.7 %reduce-scatter.2.cloned.1.call-start = ((), (), s32[]{:S(2)}) async-start(), calls=%async_computation.3 | async-start | bytes 1769472 | tf_op jit(solution)/shard_map/reduce_scatter | solution.py:101
  210.2 41.1 %copy-start.2 = (bf16[128,1,16,64]{0,3,2,1:T(8,128)(2,1)S(1)}, bf16[128,1,16,64]{0,3,2,1:T(8,128)(2,1)}, u32[]{:S(2)}) copy-start(bf16[128,1,16,64]{0,3,2,1:T(8,128)(2,1)} %param.15) | copy-start | bytes 786436
  246.5 7.4 %copy-start.1 = (bf16[128,1,128]{2,0,1:T(8,128)(2,1)S(1)}, bf16[128,1,128]{2,0,1:T(8,128)(2,1)}, u32[]{:S(2)}) copy-start(bf16[128,1,128]{2,0,1:T(8,128)(2,1)} %param.18) | copy-start | bytes 98308
  246.5 7.4 %copy-start.5 = (f32[128,1,128]{2,1,0:T(1,128)S(1)}, f32[128,1,128]{2,1,0:T(1,128)}, u32[]{:S(2)}) copy-start(f32[128,1,128]{2,1,0:T(1,128)} %param.19) | copy-start | bytes 196612
  246.5 7.4 %copy-start.6 = (f32[128,1,128]{2,1,0:T(1,128)S(1)}, f32[128,1,128]{2,1,0:T(1,128)}, u32[]{:S(2)}) copy-start(f32[128,1,128]{2,1,0:T(1,128)} %param.20) | copy-start | bytes 196612
  248.6 5.4 %slice-start = ((f32[192,1,1152]{2,1,0:T(1,128)}), f32[192,1,128]{2,1,0:T(1,128)S(1)}, s32[]{:S(2)}) async-start(f32[192,1,1152]{2,1,0:T(1,128)} %all_to_all.21), calls=%async_computation.4 | async-start | bytes 196608 | tf_op jit(solution)/shard_map/slice | solution.py:136
Sparse Core Ops, SparseCore 0:
  190.5 39.4 reduce-scatter.1
where the time goes:
time: 263 us; the launch traced here: 262 us
  starting transfers between devices  120 us (46%)
  waiting for transfers between devices  54 us (21%)
  blocking collectives  38 us (14%)
  local copies, waits for them, and re-layouts  16.4 us (6%)
  between operations  14.8 us (6%)
  matrix products  12.2 us (5%)
  other arithmetic  6.9 us (3%)
    ppermute x18, starting transfers between devices, gather_along(): got.append(lax.ppermute(piece, axis, pairs))  93.5 us
    psum x1, blocking collectives, shards(): down_sum = lax.psum(down_part, 'mp')  22.7 us
    reduce_scatter x1, waiting for transfers between devices, shards(): lax.psum_scatter(frozen_part, 'mp', scatter_dimension=1, tiled=True)  19.9 us
    ppermute x18, waiting for transfers between devices, gather_along(): got.append(lax.ppermute(piece, axis, pairs))  19.3 us
    all_to_all x1, starting transfers between devices, shards(): lax.all_to_all(sent, ADAPTER, split_axis=0, concat_axis=0, tiled=True)  15.8 us
    all_gather x1, blocking collectives, shards(): masked_full = lax.all_gather(masked_own, 'mp', axis=1, tiled=True)  15.3 us
    all_to_all x1, waiting for transfers between devices, shards(): lax.all_to_all(grads, ADAPTER, split_axis=1, concat_axis=0, tiled=True)  14.7 us
    all_to_all x1, starting transfers between devices, shards(): lax.all_to_all(grads, ADAPTER, split_axis=1, concat_axis=0, tiled=True)  10.2 us
  transfers between devices with their start and end apart: 21, of which 7 were waited for; matrix products, arithmetic and copies ran while one was open for 7% of the time, Pallas kernels for 0%

commit v1 on v0

--- a/solution.py
+++ b/solution.py
@@ -102,7 +102,9 @@
     down_part = jnp.einsum(
         "ntd,ndr->ntr", token_tiles, down_panel, preferred_element_type=jnp.float32
     )
-    down_sum = lax.psum(down_part, "mp")
+    down_sum = down_part
+    for hop in (1, 2, 4):
+        down_sum = down_sum + lax.ppermute(down_sum, "mp", [(dev, dev ^ hop) for dev in range(8)])
     down_portion = down_sum.astype(jnp.bfloat16)
     adapter_term = jnp.einsum(
         "ntr,nrv->ntv", down_portion, up_panel, preferred_element_type=jnp.float32

time: 263 us -> 275 us (1.046)
  starting transfers between devices: 120 us -> 128 us
  waiting for transfers between devices: 54 us -> 57.8 us
    ppermute x0 -> x3, starting transfers between devices: none -> 8.03 us  [shards(): lax.ppermute(down_sum, 'mp', [(dev, dev ^ hop) for dev in range(8)])]
  transfers between devices with their start and end apart: 21 -> 24, of which waited for: 7 -> 9; matrix products, arithmetic and copies ran while one was open for 7% -> 8% of each run, Pallas kernels for 0% -> 0%
where the time goes in v1:
time: 275 us; the launch traced here: 273 us
  starting transfers between devices  128 us (47%)
  waiting for transfers between devices  57.8 us (21%)
  blocking collectives  37.2 us (14%)
  local copies, waits for them, and re-layouts  16.3 us (6%)
  between operations  14.9 us (5%)
  matrix products  11.9 us (4%)
  other arithmetic  7.69 us (3%)
    ppermute x18, starting transfers between devices, gather_along(): got.append(lax.ppermute(piece, axis, pairs))  93.5 us
    psum x1, blocking collectives, shards(): backward_portion = lax.psum(backward_piece, 'mp').astype(jnp.bfloat16)  23.5 us
    reduce_scatter x1, waiting for transfers between devices, shards(): lax.psum_scatter(frozen_part, 'mp', scatter_dimension=1, tiled=True)  21.8 us
    ppermute x18, waiting for transfers between devices, gather_along(): got.append(lax.ppermute(piece, axis, pairs))  19.3 us
    all_to_all x1, starting transfers between devices, shards(): lax.all_to_all(sent, ADAPTER, split_axis=0, concat_axis=0, tiled=True)  15.8 us
    all_to_all x1, waiting for transfers between devices, shards(): lax.all_to_all(grads, ADAPTER, split_axis=1, concat_axis=0, tiled=True)  14.1 us
    all_gather x1, blocking collectives, shards(): masked_full = lax.all_gather(masked_own, 'mp', axis=1, tiled=True)  13.7 us
    all_to_all x1, starting transfers between devices, shards(): lax.all_to_all(grads, ADAPTER, split_axis=1, concat_axis=0, tiled=True)  10.4 us
  transfers between devices with their start and end apart: 24, of which 9 were waited for; matrix products, arithmetic and copies ran while one was open for 8% of the time, Pallas kernels for 0%

profile of v1, /device:TPU:6, one launch (start us, length us, event | category | flops | bytes accessed | tf_op | source)
XLA Modules:
  0.0 273.4 jit_solution(12529819617843777564)
XLA Ops:
  7.2 11.5 %collective-permute-start = (bf16[1024,16]{0,1:T(8,128)(2,1)}, bf16[1024,16]{0,1:T(8,128)(2,1)S(1)}, u32[]{:S(2)}, u32[]{:S(2)}) collective-permute-start(bf16[1024,16]{0,1:T(8,128)(2,1)} %param.14), channel_id=1, source_target_pairs={{0,120},{8,0},{16,8},{24,16},{32,24},{40,32},{48,40},{56,48},{64,5... | collective-permute-start | bytes 98312 | tf_op jit(solution)/shard_map/ppermute | solution.py:34
  18.7 3.4 %collective-permute-start.1 = (bf16[1024,16]{0,1:T(8,128)(2,1)}, bf16[1024,16]{0,1:T(8,128)(2,1)S(1)}, u32[]{:S(2)}, u32[]{:S(2)}) collective-permute-start(bf16[1024,16]{0,1:T(8,128)(2,1)} %param.14), channel_id=1, source_target_pairs={{0,112},{8,120},{16,0},{24,8},{32,16},{40,24},{48,32},{56,40},{64,... | collective-permute-start | bytes 98312 | tf_op jit(solution)/shard_map/ppermute | solution.py:34
  22.1 5.0 %collective-permute-start.2 = (bf16[1024,16]{0,1:T(8,128)(2,1)}, bf16[1024,16]{0,1:T(8,128)(2,1)S(1)}, u32[]{:S(2)}, u32[]{:S(2)}) collective-permute-start(bf16[1024,16]{0,1:T(8,128)(2,1)} %param.14), channel_id=1, source_target_pairs={{0,104},{8,112},{16,120},{24,0},{32,8},{40,16},{48,24},{56,32},{64... | collective-permute-start | bytes 98312 | tf_op jit(solution)/shard_map/ppermute | solution.py:34
  27.1 2.8 %collective-permute-start.3 = (bf16[1024,16]{0,1:T(8,128)(2,1)}, bf16[1024,16]{0,1:T(8,128)(2,1)S(1)}, u32[]{:S(2)}, u32[]{:S(2)}) collective-permute-start(bf16[1024,16]{0,1:T(8,128)(2,1)} %param.14), channel_id=1, source_target_pairs={{0,96},{8,104},{16,112},{24,120},{32,0},{40,8},{48,16},{56,24},{64... | collective-permute-start | bytes 98312 | tf_op jit(solution)/shard_map/ppermute | solution.py:34
  38.1 15.8 %all-to-all-start = ((bf16[64,3,1152]{2,1,0:T(4,128)(2,1)}), bf16[64,3,1152]{2,1,0:T(4,128)(2,1)S(1)}, u32[]{:S(2)}, u32[]{:S(2)}) async-start(bf16[64,3,1152]{2,1,0:T(4,128)(2,1)} %pad_maximum_fusion.1), calls=%async_computation.1 | async-start | bytes 1179648 | tf_op jit(solution)/shard_map/all_to_all | solution.py:89
  54.0 10.4 %collective-permute-start.5 = (bf16[1024,16]{0,1:T(8,128)(2,1)S(1)}, bf16[1024,16]{0,1:T(8,128)(2,1)S(1)}, u32[]{:S(2)}, u32[]{:S(2)}) collective-permute-start(bf16[1024,16]{0,1:T(8,128)(2,1)S(1)} %copy-done.4), channel_id=1, source_target_pairs={{0,80},{8,88},{16,96},{24,104},{32,112},{40,120},{48,0},{56,8},{64... | collective-permute-start | bytes 98312 | tf_op jit(solution)/shard_map/ppermute | solution.py:34
  64.4 4.3 %collective-permute-start.6 = (bf16[1024,16]{0,1:T(8,128)(2,1)S(1)}, bf16[1024,16]{0,1:T(8,128)(2,1)S(1)}, u32[]{:S(2)}, u32[]{:S(2)}) collective-permute-start(bf16[1024,16]{0,1:T(8,128)(2,1)S(1)} %copy-done.4), channel_id=1, source_target_pairs={{0,72},{8,80},{16,88},{24,96},{32,104},{40,112},{48,120},{56,0},{6... | collective-permute-start | bytes 98312 | tf_op jit(solution)/shard_map/ppermute | solution.py:34
  68.7 9.4 %collective-permute-start.7 = (bf16[1024,16]{0,1:T(8,128)(2,1)S(1)}, bf16[1024,16]{0,1:T(8,128)(2,1)S(1)}, u32[]{:S(2)}, u32[]{:S(2)}) collective-permute-start(bf16[1024,16]{0,1:T(8,128)(2,1)S(1)} %copy-done.4), channel_id=1, source_target_pairs={{0,64},{8,72},{16,80},{24,88},{32,96},{40,104},{48,112},{56,120},{... | collective-permute-start | bytes 98312 | tf_op jit(solution)/shard_map/ppermute | solution.py:34
  78.1 3.1 %collective-permute-start.8 = (bf16[1024,16]{0,1:T(8,128)(2,1)S(1)}, bf16[1024,16]{0,1:T(8,128)(2,1)S(1)}, u32[]{:S(2)}, u32[]{:S(2)}) collective-permute-start(bf16[1024,16]{0,1:T(8,128)(2,1)S(1)} %copy-done.4), channel_id=1, source_target_pairs={{0,56},{8,64},{16,72},{24,80},{32,88},{40,96},{48,104},{56,112},{6... | collective-permute-start | bytes 98312 | tf_op jit(solution)/shard_map/ppermute | solution.py:34
  81.2 10.3 %collective-permute-start.9 = (bf16[1024,16]{0,1:T(8,128)(2,1)S(1)}, bf16[1024,16]{0,1:T(8,128)(2,1)S(1)}, u32[]{:S(2)}, u32[]{:S(2)}) collective-permute-start(bf16[1024,16]{0,1:T(8,128)(2,1)S(1)} %copy-done.4), channel_id=1, source_target_pairs={{0,48},{8,56},{16,64},{24,72},{32,80},{40,88},{48,96},{56,104},{64... | collective-permute-start | bytes 98312 | tf_op jit(solution)/shard_map/ppermute | solution.py:34
  91.5 6.7 %collective-permute-start.10 = (bf16[1024,16]{0,1:T(8,128)(2,1)S(1)}, bf16[1024,16]{0,1:T(8,128)(2,1)S(1)}, u32[]{:S(2)}, u32[]{:S(2)}) collective-permute-start(bf16[1024,16]{0,1:T(8,128)(2,1)S(1)} %copy-done.4), channel_id=1, source_target_pairs={{0,40},{8,48},{16,56},{24,64},{32,72},{40,80},{48,88},{56,96},{64,... | collective-permute-start | bytes 98312 | tf_op jit(solution)/shard_map/ppermute | solution.py:34
  98.2 1.9 collective-permute-start.11
  100.2 5.2 %collective-permute-start.12 = (bf16[1024,16]{0,1:T(8,128)(2,1)S(1)}, bf16[1024,16]{0,1:T(8,128)(2,1)S(1)}, u32[]{:S(2)}, u32[]{:S(2)}) collective-permute-start(bf16[1024,16]{0,1:T(8,128)(2,1)S(1)} %copy-done.4), channel_id=1, source_target_pairs={{0,24},{8,32},{16,40},{24,48},{32,56},{40,64},{48,72},{56,80},{64,... | collective-permute-start | bytes 98312 | tf_op jit(solution)/shard_map/ppermute | solution.py:34
  105.5 2.7 collective-permute-start.13
  108.1 4.8 %collective-permute-start.14 = (bf16[1024,16]{0,1:T(8,128)(2,1)S(1)}, bf16[1024,16]{0,1:T(8,128)(2,1)S(1)}, u32[]{:S(2)}, u32[]{:S(2)}) collective-permute-start(bf16[1024,16]{0,1:T(8,128)(2,1)S(1)} %copy-done.4), channel_id=1, source_target_pairs={{0,8},{8,16},{16,24},{24,32},{32,40},{40,48},{48,56},{56,64},{64,7... | collective-permute-start | bytes 98312 | tf_op jit(solution)/shard_map/ppermute | solution.py:34
  115.4 4.8 %collective-permute-start.15 = (bf16[1024,256]{0,1:T(8,128)(2,1)S(1)}, bf16[1024,256]{0,1:T(8,128)(2,1)S(1)}, u32[]{:S(2)}, u32[]{:S(2)}) collective-permute-start(bf16[1024,256]{0,1:T(8,128)(2,1)S(1)} %bitcast.143), channel_id=1, source_target_pairs={{0,384},{128,0},{256,128},{384,256},{1,385},{129,1},{257,129},{385... | collective-permute-start | bytes 1572872 | tf_op jit(solution)/shard_map/ppermute | solution.py:34
  120.3 2.5 collective-permute-start.16
  123.0 2.9 %collective-permute-start.17 = (bf16[1024,256]{0,1:T(8,128)(2,1)S(1)}, bf16[1024,256]{0,1:T(8,128)(2,1)S(1)}, u32[]{:S(2)}, u32[]{:S(2)}) collective-permute-start(bf16[1024,256]{0,1:T(8,128)(2,1)S(1)} %bitcast.145), channel_id=1, source_target_pairs={{0,128},{128,256},{256,384},{384,0},{1,129},{129,257},{257,385},{3... | collective-permute-start | bytes 1572872 | tf_op jit(solution)/shard_map/ppermute | solution.py:34
  125.9 11.5 %collective-permute-done.15 = bf16[1024,256]{0,1:T(8,128)(2,1)S(1)} collective-permute-done((bf16[1024,256]{0,1:T(8,128)(2,1)S(1)}, bf16[1024,256]{0,1:T(8,128)(2,1)S(1)}, u32[]{:S(2)}, u32[]{:S(2)}) %collective-permute-start.15) | collective-permute-done | bytes 524320 | tf_op jit(solution)/shard_map/ppermute | solution.py:34
  137.6 5.5 %collective-permute-done.17 = bf16[1024,256]{0,1:T(8,128)(2,1)S(1)} collective-permute-done((bf16[1024,256]{0,1:T(8,128)(2,1)S(1)}, bf16[1024,256]{0,1:T(8,128)(2,1)S(1)}, u32[]{:S(2)}, u32[]{:S(2)}) %collective-permute-start.17) | collective-permute-done | bytes 524320 | tf_op jit(solution)/shard_map/ppermute | solution.py:34
  146.2 1.9 collective-permute-start.18
  149.4 2.7 %collective-permute-start.19 = (f32[3,128,64]{1,2,0:T(8,128)S(1)}, f32[3,128,64]{1,2,0:T(8,128)S(1)}, u32[]{:S(2)}, u32[]{:S(2)}) collective-permute-start(f32[3,128,64]{1,2,0:T(8,128)S(1)} %add.84), channel_id=1, source_target_pairs={{0,2},{1,3},{2,0},{3,1},{4,6},{5,7},{6,4},{7,5},{8,10},{9,11},{10,... | collective-permute-start | bytes 294920 | tf_op jit(solution)/shard_map/ppermute | solution.py:107
  152.1 23.5 %psum.7 = bf16[3,128,64]{1,2,0:T(8,128)(2,1)S(1)} all-reduce(f32[3,128,64]{1,2,0:T(8,128)S(1)} %convolution_multiply_fusion.2), channel_id=1, replica_groups=mesh['ay'=4,'az'=16,'mp'=8] {'mp'}, use_global_device_ids=true, to_apply=%region_2.3 | all-reduce | flops 24576 | bytes 147456 | tf_op jit(solution)/shard_map/psum | solution.py:119
  175.7 3.4 %collective-permute-start.20 = (f32[3,128,64]{1,2,0:T(8,128)S(1)}, f32[3,128,64]{1,2,0:T(8,128)}, u32[]{:S(2)}, u32[]{:S(2)}) collective-permute-start(f32[3,128,64]{1,2,0:T(8,128)S(1)} %add.85), channel_id=1, source_target_pairs={{0,4},{1,5},{2,6},{3,7},{4,0},{5,1},{6,2},{7,3},{8,12},{9,13},{10,... | collective-permute-start | bytes 294920 | tf_op jit(solution)/shard_map/ppermute | solution.py:107
  188.4 10.4 %all-to-all-start.1 = ((f32[3,64,1152]{2,0,1:T(4,128)}), f32[3,64,1152]{2,0,1:T(4,128)S(1)}, u32[]{:S(2)}, u32[]{:S(2)}) async-start(f32[3,64,1152]{2,0,1:T(4,128)} %copy.83), calls=%async_computation.2 | async-start | bytes 2359296 | tf_op jit(solution)/shard_map/all_to_all | solution.py:136
  198.8 4.0 %convolution_bitcast_fusion = f32[384,1024]{0,1:T(8,128)} fusion(bf16[1024,1024]{0,1:T(8,128)(2,1)} %bitcast.150, bf16[384,1024]{1,0:T(8,128)(2,1)S(1)} %copy-done), kind=kOutput, calls=%fused_computation.4 | convolution fusion | flops 805306368 | bytes 4456448 | tf_op jit(solution)/shard_map/dot_general | solution.py:100
  202.9 13.7 %all_gather.3 = bf16[384,1024]{1,0:T(8,128)(2,1)S(1)} all-gather(bf16[384,128]{1,0:T(8,128)(2,1)S(1)} %broadcast_multiply_fusion), channel_id=1, replica_groups=mesh['ay'=4,'az'=16,'mp'=8] {'mp'}, dimensions={1}, use_global_device_ids=true | all-gather | bytes 884736 | tf_op jit(solution)/shard_map/all_gather | solution.py:82
  217.0 3.5 %fusion = bf16[384,1024]{1,0:T(8,128)(2,1)} fusion(f32[3,128,1024]{2,1,0:T(8,128)S(1)} %fusion.17, bf16[384,1024]{1,0:T(8,128)(2,1)S(1)} %all_gather.3, bf16[1024,1024]{0,1:T(8,128)(2,1)} %bitcast.151), kind=kOutput, calls=%fused_computation.3 | convolution fusion | flops 806092800 | bytes 5242880 | tf_op jit(solution)/shard_map/dot_general | solution.py:120
  220.8 21.8 %reduce-scatter.2.cloned.1.call-done = f32[384,128]{0,1:T(8,128)} async-done(((f32[384,1024]{0,1:T(8,128)}), f32[384,128]{0,1:T(8,128)}) %reduce-scatter.2.cloned.1.call-update) | async-done | bytes 196624 | tf_op jit(solution)/shard_map/reduce_scatter | solution.py:101
  244.3 14.1 %all-to-all-done.1 = f32[3,64,1152]{2,0,1:T(4,128)S(1)} async-done(((f32[3,64,1152]{2,0,1:T(4,128)}), f32[3,64,1152]{2,0,1:T(4,128)S(1)}, u32[]{:S(2)}, u32[]{:S(2)}) %all-to-all-start.1) | async-done | bytes 884768 | tf_op jit(solution)/shard_map/all_to_all | solution.py:136
  258.4 2.0 all_to_all.21
  263.2 2.4 divide_subtract_fusion
  (120 shorter events, 30.8 us)
Async XLA Ops:
  7.2 138.6 %copy-start = (bf16[384,1024]{1,0:T(8,128)(2,1)S(1)}, bf16[384,1024]{1,0:T(8,128)(2,1)}, u32[]{:S(2)}) copy-start(bf16[384,1024]{1,0:T(8,128)(2,1)} %param.12) | copy-start | bytes 2359300
  7.2 46.7 %copy-start.4 = (bf16[1024,16]{0,1:T(8,128)(2,1)S(1)}, bf16[1024,16]{0,1:T(8,128)(2,1)}, u32[]{:S(2)}) copy-start(bf16[1024,16]{0,1:T(8,128)(2,1)} %param.14) | copy-start | bytes 98308
  7.2 46.7 %copy-start.8 = (s32[192]{0:T(256)S(1)}, s32[192]{0:T(256)}, u32[]{:S(2)}) copy-start(s32[192]{0:T(256)} %param.22) | copy-start | bytes 2308
  7.2 46.8 %collective-permute-start = (bf16[1024,16]{0,1:T(8,128)(2,1)}, bf16[1024,16]{0,1:T(8,128)(2,1)S(1)}, u32[]{:S(2)}, u32[]{:S(2)}) collective-permute-start(bf16[1024,16]{0,1:T(8,128)(2,1)} %param.14), channel_id=1, source_target_pairs={{0,120},{8,0},{16,8},{24,16},{32,24},{40,32},{48,40},{56,48},{64,5... | collective-permute-start | bytes 98312 | tf_op jit(solution)/shard_map/ppermute | solution.py:34
  18.7 45.6 %collective-permute-start.1 = (bf16[1024,16]{0,1:T(8,128)(2,1)}, bf16[1024,16]{0,1:T(8,128)(2,1)S(1)}, u32[]{:S(2)}, u32[]{:S(2)}) collective-permute-start(bf16[1024,16]{0,1:T(8,128)(2,1)} %param.14), channel_id=1, source_target_pairs={{0,112},{8,120},{16,0},{24,8},{32,16},{40,24},{48,32},{56,40},{64,... | collective-permute-start | bytes 98312 | tf_op jit(solution)/shard_map/ppermute | solution.py:34
  22.1 46.6 %collective-permute-start.2 = (bf16[1024,16]{0,1:T(8,128)(2,1)}, bf16[1024,16]{0,1:T(8,128)(2,1)S(1)}, u32[]{:S(2)}, u32[]{:S(2)}) collective-permute-start(bf16[1024,16]{0,1:T(8,128)(2,1)} %param.14), channel_id=1, source_target_pairs={{0,104},{8,112},{16,120},{24,0},{32,8},{40,16},{48,24},{56,32},{64... | collective-permute-start | bytes 98312 | tf_op jit(solution)/shard_map/ppermute | solution.py:34
  27.1 51.0 %collective-permute-start.3 = (bf16[1024,16]{0,1:T(8,128)(2,1)}, bf16[1024,16]{0,1:T(8,128)(2,1)S(1)}, u32[]{:S(2)}, u32[]{:S(2)}) collective-permute-start(bf16[1024,16]{0,1:T(8,128)(2,1)} %param.14), channel_id=1, source_target_pairs={{0,96},{8,104},{16,112},{24,120},{32,0},{40,8},{48,16},{56,24},{64... | collective-permute-start | bytes 98312 | tf_op jit(solution)/shard_map/ppermute | solution.py:34
  30.0 51.2 %collective-permute-start.4 = (bf16[1024,16]{0,1:T(8,128)(2,1)}, bf16[1024,16]{0,1:T(8,128)(2,1)S(1)}, u32[]{:S(2)}, u32[]{:S(2)}) collective-permute-start(bf16[1024,16]{0,1:T(8,128)(2,1)} %param.14), channel_id=1, source_target_pairs={{0,88},{8,96},{16,104},{24,112},{32,120},{40,0},{48,8},{56,16},{64... | collective-permute-start | bytes 98312 | tf_op jit(solution)/shard_map/ppermute | solution.py:34
  34.2 88.7 %copy-start.5 = (bf16[384,128]{1,0:T(8,128)(2,1)S(1)}, bf16[384,128]{1,0:T(8,128)(2,1)}, u32[]{:S(2)}) copy-start(bf16[384,128]{1,0:T(8,128)(2,1)} %param.13) | copy-start | bytes 294916
  38.1 106.8 %all-to-all-start = ((bf16[64,3,1152]{2,1,0:T(4,128)(2,1)}), bf16[64,3,1152]{2,1,0:T(4,128)(2,1)S(1)}, u32[]{:S(2)}, u32[]{:S(2)}) async-start(bf16[64,3,1152]{2,1,0:T(4,128)(2,1)} %pad_maximum_fusion.1), calls=%async_computation.1 | async-start | bytes 1179648 | tf_op jit(solution)/shard_map/all_to_all | solution.py:89
  54.0 37.5 %collective-permute-start.5 = (bf16[1024,16]{0,1:T(8,128)(2,1)S(1)}, bf16[1024,16]{0,1:T(8,128)(2,1)S(1)}, u32[]{:S(2)}, u32[]{:S(2)}) collective-permute-start(bf16[1024,16]{0,1:T(8,128)(2,1)S(1)} %copy-done.4), channel_id=1, source_target_pairs={{0,80},{8,88},{16,96},{24,104},{32,112},{40,120},{48,0},{56,8},{64... | collective-permute-start | bytes 98312 | tf_op jit(solution)/shard_map/ppermute | solution.py:34
  64.4 33.8 %collective-permute-start.6 = (bf16[1024,16]{0,1:T(8,128)(2,1)S(1)}, bf16[1024,16]{0,1:T(8,128)(2,1)S(1)}, u32[]{:S(2)}, u32[]{:S(2)}) collective-permute-start(bf16[1024,16]{0,1:T(8,128)(2,1)S(1)} %copy-done.4), channel_id=1, source_target_pairs={{0,72},{8,80},{16,88},{24,96},{32,104},{40,112},{48,120},{56,0},{6... | collective-permute-start | bytes 98312 | tf_op jit(solution)/shard_map/ppermute | solution.py:34
  68.7 31.5 %collective-permute-start.7 = (bf16[1024,16]{0,1:T(8,128)(2,1)S(1)}, bf16[1024,16]{0,1:T(8,128)(2,1)S(1)}, u32[]{:S(2)}, u32[]{:S(2)}) collective-permute-start(bf16[1024,16]{0,1:T(8,128)(2,1)S(1)} %copy-done.4), channel_id=1, source_target_pairs={{0,64},{8,72},{16,80},{24,88},{32,96},{40,104},{48,112},{56,120},{... | collective-permute-start | bytes 98312 | tf_op jit(solution)/shard_map/ppermute | solution.py:34
  78.1 27.3 %collective-permute-start.8 = (bf16[1024,16]{0,1:T(8,128)(2,1)S(1)}, bf16[1024,16]{0,1:T(8,128)(2,1)S(1)}, u32[]{:S(2)}, u32[]{:S(2)}) collective-permute-start(bf16[1024,16]{0,1:T(8,128)(2,1)S(1)} %copy-done.4), channel_id=1, source_target_pairs={{0,56},{8,64},{16,72},{24,80},{32,88},{40,96},{48,104},{56,112},{6... | collective-permute-start | bytes 98312 | tf_op jit(solution)/shard_map/ppermute | solution.py:34
  81.2 26.9 %collective-permute-start.9 = (bf16[1024,16]{0,1:T(8,128)(2,1)S(1)}, bf16[1024,16]{0,1:T(8,128)(2,1)S(1)}, u32[]{:S(2)}, u32[]{:S(2)}) collective-permute-start(bf16[1024,16]{0,1:T(8,128)(2,1)S(1)} %copy-done.4), channel_id=1, source_target_pairs={{0,48},{8,56},{16,64},{24,72},{32,80},{40,88},{48,96},{56,104},{64... | collective-permute-start | bytes 98312 | tf_op jit(solution)/shard_map/ppermute | solution.py:34
  91.5 21.4 %collective-permute-start.10 = (bf16[1024,16]{0,1:T(8,128)(2,1)S(1)}, bf16[1024,16]{0,1:T(8,128)(2,1)S(1)}, u32[]{:S(2)}, u32[]{:S(2)}) collective-permute-start(bf16[1024,16]{0,1:T(8,128)(2,1)S(1)} %copy-done.4), channel_id=1, source_target_pairs={{0,40},{8,48},{16,56},{24,64},{32,72},{40,80},{48,88},{56,96},{64,... | collective-permute-start | bytes 98312 | tf_op jit(solution)/shard_map/ppermute | solution.py:34
  98.2 14.7 %collective-permute-start.11 = (bf16[1024,16]{0,1:T(8,128)(2,1)S(1)}, bf16[1024,16]{0,1:T(8,128)(2,1)S(1)}, u32[]{:S(2)}, u32[]{:S(2)}) collective-permute-start(bf16[1024,16]{0,1:T(8,128)(2,1)S(1)} %copy-done.4), channel_id=1, source_target_pairs={{0,32},{8,40},{16,48},{24,56},{32,64},{40,72},{48,80},{56,88},{64,... | collective-permute-start | bytes 98312 | tf_op jit(solution)/shard_map/ppermute | solution.py:34
  100.2 12.8 %collective-permute-start.12 = (bf16[1024,16]{0,1:T(8,128)(2,1)S(1)}, bf16[1024,16]{0,1:T(8,128)(2,1)S(1)}, u32[]{:S(2)}, u32[]{:S(2)}) collective-permute-start(bf16[1024,16]{0,1:T(8,128)(2,1)S(1)} %copy-done.4), channel_id=1, source_target_pairs={{0,24},{8,32},{16,40},{24,48},{32,56},{40,64},{48,72},{56,80},{64,... | collective-permute-start | bytes 98312 | tf_op jit(solution)/shard_map/ppermute | solution.py:34
  105.5 7.9 %collective-permute-start.13 = (bf16[1024,16]{0,1:T(8,128)(2,1)S(1)}, bf16[1024,16]{0,1:T(8,128)(2,1)S(1)}, u32[]{:S(2)}, u32[]{:S(2)}) collective-permute-start(bf16[1024,16]{0,1:T(8,128)(2,1)S(1)} %copy-done.4), channel_id=1, source_target_pairs={{0,16},{8,24},{16,32},{24,40},{32,48},{40,56},{48,64},{56,72},{64,... | collective-permute-start | bytes 98312 | tf_op jit(solution)/shard_map/ppermute | solution.py:34
  108.1 7.0 %collective-permute-start.14 = (bf16[1024,16]{0,1:T(8,128)(2,1)S(1)}, bf16[1024,16]{0,1:T(8,128)(2,1)S(1)}, u32[]{:S(2)}, u32[]{:S(2)}) collective-permute-start(bf16[1024,16]{0,1:T(8,128)(2,1)S(1)} %copy-done.4), channel_id=1, source_target_pairs={{0,8},{8,16},{16,24},{24,32},{32,40},{40,48},{48,56},{56,64},{64,7... | collective-permute-start | bytes 98312 | tf_op jit(solution)/shard_map/ppermute | solution.py:34
  115.4 22.0 %collective-permute-start.15 = (bf16[1024,256]{0,1:T(8,128)(2,1)S(1)}, bf16[1024,256]{0,1:T(8,128)(2,1)S(1)}, u32[]{:S(2)}, u32[]{:S(2)}) collective-permute-start(bf16[1024,256]{0,1:T(8,128)(2,1)S(1)} %bitcast.143), channel_id=1, source_target_pairs={{0,384},{128,0},{256,128},{384,256},{1,385},{129,1},{257,129},{385... | collective-permute-start | bytes 1572872 | tf_op jit(solution)/shard_map/ppermute | solution.py:34
  120.3 17.2 %collective-permute-start.16 = (bf16[1024,256]{0,1:T(8,128)(2,1)S(1)}, bf16[1024,256]{0,1:T(8,128)(2,1)S(1)}, u32[]{:S(2)}, u32[]{:S(2)}) collective-permute-start(bf16[1024,256]{0,1:T(8,128)(2,1)S(1)} %bitcast.144), channel_id=1, source_target_pairs={{0,256},{128,384},{256,0},{384,128},{1,257},{129,385},{257,1},{385... | collective-permute-start | bytes 1572872 | tf_op jit(solution)/shard_map/ppermute | solution.py:34
  123.0 20.1 %collective-permute-start.17 = (bf16[1024,256]{0,1:T(8,128)(2,1)S(1)}, bf16[1024,256]{0,1:T(8,128)(2,1)S(1)}, u32[]{:S(2)}, u32[]{:S(2)}) collective-permute-start(bf16[1024,256]{0,1:T(8,128)(2,1)S(1)} %bitcast.145), channel_id=1, source_target_pairs={{0,128},{128,256},{256,384},{384,0},{1,129},{129,257},{257,385},{3... | collective-permute-start | bytes 1572872 | tf_op jit(solution)/shard_map/ppermute | solution.py:34
  146.2 3.2 %collective-permute-start.18 = (f32[3,128,64]{1,2,0:T(8,128)S(1)}, f32[3,128,64]{1,2,0:T(8,128)S(1)}, u32[]{:S(2)}, u32[]{:S(2)}) collective-permute-start(f32[3,128,64]{1,2,0:T(8,128)S(1)} %convolution_bitcast_fusion.2), channel_id=1, source_target_pairs={{0,1},{1,0},{2,3},{3,2},{4,5},{5,4},{6,7},{7,6},{8,9},{9,8},{10,11... | collective-permute-start | bytes 294920 | tf_op jit(solution)/shard_map/ppermute | solution.py:107
  149.4 26.2 %collective-permute-start.19 = (f32[3,128,64]{1,2,0:T(8,128)S(1)}, f32[3,128,64]{1,2,0:T(8,128)S(1)}, u32[]{:S(2)}, u32[]{:S(2)}) collective-permute-start(f32[3,128,64]{1,2,0:T(8,128)S(1)} %add.84), channel_id=1, source_target_pairs={{0,2},{1,3},{2,0},{3,1},{4,6},{5,7},{6,4},{7,5},{8,10},{9,11},{10,... | collective-permute-start | bytes 294920 | tf_op jit(solution)/shard_map/ppermute | solution.py:107
  175.7 8.9 %collective-permute-start.20 = (f32[3,128,64]{1,2,0:T(8,128)S(1)}, f32[3,128,64]{1,2,0:T(8,128)}, u32[]{:S(2)}, u32[]{:S(2)}) collective-permute-start(f32[3,128,64]{1,2,0:T(8,128)S(1)} %add.85), channel_id=1, source_target_pairs={{0,4},{1,5},{2,6},{3,7},{4,0},{5,1},{6,2},{7,3},{8,12},{9,13},{10,... | collective-permute-start | bytes 294920 | tf_op jit(solution)/shard_map/ppermute | solution.py:107
  188.4 70.0 %all-to-all-start.1 = ((f32[3,64,1152]{2,0,1:T(4,128)}), f32[3,64,1152]{2,0,1:T(4,128)S(1)}, u32[]{:S(2)}, u32[]{:S(2)}) async-start(f32[3,64,1152]{2,0,1:T(4,128)} %copy.83), calls=%async_computation.2 | async-start | bytes 2359296 | tf_op jit(solution)/shard_map/all_to_all | solution.py:136
  198.8 43.8 %reduce-scatter.2.cloned.1.call-start = ((), (), s32[]{:S(2)}) async-start(), calls=%async_computation.3 | async-start | bytes 1769472 | tf_op jit(solution)/shard_map/reduce_scatter | solution.py:101
  220.4 42.8 %copy-start.2 = (bf16[128,1,16,64]{0,3,2,1:T(8,128)(2,1)S(1)}, bf16[128,1,16,64]{0,3,2,1:T(8,128)(2,1)}, u32[]{:S(2)}) copy-start(bf16[128,1,16,64]{0,3,2,1:T(8,128)(2,1)} %param.15) | copy-start | bytes 786436
  220.4 42.8 %copy-start.3 = (f32[128,1,16,64]{0,3,2,1:T(8,128)S(1)}, f32[128,1,16,64]{0,3,2,1:T(8,128)}, u32[]{:S(2)}) copy-start(f32[128,1,16,64]{0,3,2,1:T(8,128)} %param.16) | copy-start | bytes 1572868
  258.4 7.2 %copy-start.6 = (f32[128,1,128]{2,1,0:T(1,128)S(1)}, f32[128,1,128]{2,1,0:T(1,128)}, u32[]{:S(2)}) copy-start(f32[128,1,128]{2,1,0:T(1,128)} %param.19) | copy-start | bytes 196612
  258.4 7.2 %copy-start.7 = (f32[128,1,128]{2,1,0:T(1,128)S(1)}, f32[128,1,128]{2,1,0:T(1,128)}, u32[]{:S(2)}) copy-start(f32[128,1,128]{2,1,0:T(1,128)} %param.20) | copy-start | bytes 196612
  (2 other events, 12.4 us)
Sparse Core Ops, SparseCore 0:
  203.0 39.5 reduce-scatter.1
